TPU v7x, 128 devices: a whole 4x4x4 slice. The times are simulated.
128 devices in a mesh: row: 8 (over z, core), col: 8 (over y_lo, x), dep: 2 (over y_hi).
Axes of the slice: x: 4, y: 4 (y_hi: 2, y_lo: 2; y = y_hi * 2 + y_lo), z: 4, core: 2. Of those that a mesh axis runs over, the one named last changes fastest.
Arguments:
- tokens: bfloat16 [2048, 8192], P(('dep', 'col'), 'row'), may hold values from -6 to 6
- gate_weight: bfloat16 [8192, 14336], P('row', 'col'), may hold values from -0.0625 to 0.0625
- up_weight: bfloat16 [8192, 14336], P('row', 'col'), may hold values from -0.0625 to 0.0625
- cotangent: bfloat16 [2048, 14336], P(('dep', 'row'), 'col'), may hold values from -6 to 6
Outputs:
- hidden: bfloat16 [2048, 14336], P(('dep', 'row'), 'col')
- grad_tokens: bfloat16 [2048, 8192], P(('dep', 'col'), 'row')
- grad_gate_weight: bfloat16 [8192, 14336], P('row', ('col', 'dep'))
- grad_up_weight: bfloat16 [8192, 14336], P('row', ('col', 'dep'))
All inputs are finite; a program needn't handle non-finite values.
Results may differ from a plain program's by a relative error of at most 0.02.
Values may be sent and summed in bfloat16 or wider, within the bound.
No kernel may reach another device: no remote copies, remote signals or barrier semaphores. Data moves between devices by JAX's collectives and lax.ppermute only.
A program may use at most 128 MiB of HBM per device.

v0:
```python
import jax
import jax.numpy as jnp
from jax import lax
from jax.sharding import PartitionSpec as P


def halves(x, dep, half):
    own = lax.dynamic_slice_in_dim(x, dep * half, half, axis=1)
    other = lax.dynamic_slice_in_dim(x, (1 - dep) * half, half, axis=1)
    return (own, other)


def on_device(tokens, gate_weight, up_weight, cotangent):
    width = gate_weight.shape[1]
    half = width // 2
    dep = lax.axis_index("dep")
    n_col = lax.axis_size("col")
    contract = (((0,), (0,)), ((), ()))
    transposed = (((1,), (1,)), ((), ()))
    pair = [(0, 1), (1, 0)]

    def gather_col(block):
        return lax.all_to_all(jnp.tile(block, (n_col, 1)), "col", 0, 0, tiled=True)

    partner_tokens = lax.ppermute(tokens, "dep", pair)
    gathered = gather_col(tokens)
    first = jnp.dot(gathered, gate_weight, preferred_element_type=jnp.float32)
    second = jnp.dot(gathered, up_weight, preferred_element_type=jnp.float32)
    joined = lax.psum_scatter(
        jnp.concatenate([first, second], axis=1).astype(jnp.bfloat16),
        "row",
        scatter_dimension=0,
        tiled=True,
    )
    gathered_partner = gather_col(partner_tokens)
    joined, gathered_partner = lax.optimization_barrier((joined, gathered_partner))
    gate = joined[:, :width]
    up = joined[:, width:]
    upstream = cotangent

    def grads(gate, up, upstream):
        gate, up, upstream = (x.astype(jnp.float32) for x in (gate, up, upstream))
        sigma = jax.nn.sigmoid(gate)
        active = gate * sigma
        grad_gate = (upstream * up * sigma * (1.0 + gate * (1.0 - sigma))).astype(jnp.bfloat16)
        return (grad_gate, (upstream * active).astype(jnp.bfloat16))

    gate_own, gate_other = halves(gate, dep, half)
    up_own, up_other = halves(up, dep, half)
    up_stream_own, up_stream_other = halves(upstream, dep, half)
    grad_gate_other, grad_up_other = grads(gate_other, up_other, up_stream_other)
    payload = jnp.concatenate([grad_gate_other, grad_up_other], axis=1)
    payload, gate_own, up_own, up_stream_own, gate, up = lax.optimization_barrier(
        (payload, gate_own, up_own, up_stream_own, gate, up)
    )
    partner_gate, partner_up = jnp.split(lax.ppermute(payload, "dep", pair), 2, axis=1)
    grad_gate_own, grad_up_own = grads(gate_own, up_own, up_stream_own)
    gate, up = (gate.astype(jnp.float32), up.astype(jnp.float32))
    hidden = (gate * jax.nn.sigmoid(gate) * up).astype(jnp.bfloat16)
    gate_own, up_own, gate_other, up_other = (
        grad_gate_own,
        grad_up_own,
        grad_gate_other,
        grad_up_other,
    )
    full = lax.all_gather(
        jnp.concatenate([gate_own, up_own, gate_other, up_other, partner_gate, partner_up], axis=1),
        "row",
        axis=0,
        tiled=True,
    )
    wg_own, wg_other = halves(gate_weight, dep, half)
    wu_own, wu_other = halves(up_weight, dep, half)
    weights = jnp.concatenate([wg_own, wu_own, wg_other, wu_other], axis=1)
    term = lax.dot_general(
        full[:, : 2 * width], weights, transposed, preferred_element_type=jnp.float32
    )
    term = term.astype(jnp.bfloat16).reshape(n_col, -1, term.shape[1])
    term, gathered, gathered_partner = lax.optimization_barrier((term, gathered, gathered_partner))
    parts = lax.all_to_all(term, "col", 0, 0, tiled=True)
    grad_tokens = parts.astype(jnp.float32).sum(axis=0).astype(jnp.bfloat16)

    def weight_grad(own, partner):
        mine = lax.dot_general(gathered, own, contract, preferred_element_type=jnp.float32)
        theirs = lax.dot_general(
            gathered_partner, partner, contract, preferred_element_type=jnp.float32
        )
        return (
            mine.astype(jnp.bfloat16).astype(jnp.float32)
            + theirs.astype(jnp.bfloat16).astype(jnp.float32)
        ).astype(jnp.bfloat16)

    sum_gate = weight_grad(full[:, :half], full[:, 2 * width : 2 * width + half])
    sum_up = weight_grad(full[:, half:width], full[:, 2 * width + half :])
    return (hidden, grad_tokens, sum_gate, sum_up)


def solution(mesh):
    return jax.shard_map(
        on_device,
        mesh=mesh,
        in_specs=(
            P(("dep", "col"), "row"),
            P("row", "col"),
            P("row", "col"),
            P(("dep", "row"), "col"),
        ),
        out_specs=(
            P(("dep", "row"), "col"),
            P(("dep", "col"), "row"),
            P("row", ("col", "dep")),
            P("row", ("col", "dep")),
        ),
        check_vma=False,
    )
```

profile of v0, /device:TPU:6, one launch (start us, length us, event | category | flops | bytes accessed | tf_op | source)
XLA Modules:
  0.0 237.5 jit_solution(15468545211119573866)
XLA Ops:
  7.2 0.0 reduce-scatter.2.cloned.1.call-start
  7.2 1.2 tile.4
  8.4 0.0 copy-start
  8.4 30.9 %all_to_all.23 = bf16[8,128,1024]{2,1,0:T(8,128)(2,1)S(1)} all-to-all(bf16[8,128,1024]{2,1,0:T(8,128)(2,1)S(1)} %tile.4), channel_id=1, replica_groups=mesh['row'=8,'col'=8,'dep'=2] {'col'}, dimensions={0} | all-to-all | bytes 4194304 | tf_op jit(solution)/shard_map/all_to_all | solution.py:23
  39.4 0.0 copy-start.2
  39.4 0.0 copy-done
  39.4 0.0 copy-start.1
  39.4 4.2 %convolution_convert_fusion = bf16[1024,1792]{1,0:T(8,128)(2,1)S(1)} fusion(bf16[1024,1024]{1,0:T(8,128)(2,1)S(1)} %bitcast.11, bf16[1024,1792]{1,0:T(8,128)(2,1)S(1)} %copy-done), kind=kOutput, calls=%fused_computation.10 | convolution fusion | flops 3759931392 | bytes 9437184 | tf_op jit(solution)/shard_map/dot_general | solution.py:28
  43.5 0.0 copy-done.2
  43.5 0.0 copy-done.1
  43.5 5.4 %convolution_convert_fusion.1 = bf16[1024,1792]{1,0:T(8,128)(2,1)} fusion(bf16[1024,1024]{1,0:T(8,128)(2,1)S(1)} %bitcast.12, bf16[1024,1792]{1,0:T(8,128)(2,1)S(1)} %copy-done.1), kind=kOutput, calls=%fused_computation.11 | convolution fusion | flops 3759931392 | bytes 9437184 | tf_op jit(solution)/shard_map/dot_general | solution.py:27
  48.9 5.5 %pad_maximum_fusion = bf16[1024,3584]{1,0:T(8,128)(2,1)} fusion(bf16[1024,1792]{1,0:T(8,128)(2,1)S(1)} %convolution_convert_fusion, bf16[1024,1792]{1,0:T(8,128)(2,1)} %convolution_convert_fusion.1), kind=kLoop, calls=%fused_computation.2 | loop fusion | flops 14680064 | bytes 14680064 | tf_op jit(solution)/shard_map/concatenate | solution.py:30
  54.5 0.0 copy-start.7
  54.5 0.0 reduce-scatter.2.cloned.1.call-update
  54.5 0.9 copy-done.7
  55.4 2.9 %collective-permute-start = (bf16[128,1024]{1,0:T(8,128)(2,1)S(1)}, bf16[128,1024]{1,0:T(8,128)(2,1)S(1)}, u32[]{:S(2)}, u32[]{:S(2)}) collective-permute-start(bf16[128,1024]{1,0:T(8,128)(2,1)S(1)} %copy-done.7), channel_id=1, source_target_pairs={{0,1},{1,0},{2,3},{3,2},{4,5},{5,4},{6,7},{7,6},{8,9},{9,8},{10,11... | collective-permute-start | bytes 786440 | tf_op jit(solution)/shard_map/ppermute | solution.py:25
  58.3 5.2 %collective-permute-done = bf16[128,1024]{1,0:T(8,128)(2,1)S(1)} collective-permute-done((bf16[128,1024]{1,0:T(8,128)(2,1)S(1)}, bf16[128,1024]{1,0:T(8,128)(2,1)S(1)}, u32[]{:S(2)}, u32[]{:S(2)}) %collective-permute-start) | collective-permute-done | bytes 262176 | tf_op jit(solution)/shard_map/ppermute | solution.py:25
  63.5 1.6 tile.5
  65.1 5.9 %all-to-all-start.1 = ((bf16[8,128,1024]{2,1,0:T(8,128)(2,1)}), bf16[8,128,1024]{2,1,0:T(8,128)(2,1)S(1)}, u32[]{:S(2)}, u32[]{:S(2)}) async-start(bf16[8,128,1024]{2,1,0:T(8,128)(2,1)} %tile.5), calls=%async_computation.2 | async-start | bytes 4194304 | tf_op jit(solution)/shard_map/all_to_all | solution.py:23
  71.1 0.0 all-gather.2.cloned.1.call-start
  71.1 0.0 copy-done.6
  71.1 22.6 %all-to-all-done.1 = bf16[8,128,1024]{2,1,0:T(8,128)(2,1)S(1)} async-done(((bf16[8,128,1024]{2,1,0:T(8,128)(2,1)}), bf16[8,128,1024]{2,1,0:T(8,128)(2,1)S(1)}, u32[]{:S(2)}, u32[]{:S(2)}) %all-to-all-start.1) | async-done | bytes 2097184 | tf_op jit(solution)/shard_map/all_to_all | solution.py:23
  93.7 10.4 %reduce-scatter.2.cloned.1.call-done = bf16[128,3584]{1,0:T(8,128)(2,1)} async-done(((bf16[1024,3584]{1,0:T(8,128)(2,1)}), bf16[128,3584]{1,0:T(8,128)(2,1)}) %reduce-scatter.2.cloned.1.call-update) | async-done | bytes 917520 | tf_op jit(solution)/shard_map/reduce_scatter | solution.py:29
  104.1 0.0 copy-done.4
  104.1 1.2 fusion.50
  105.4 0.3 fusion.33
  105.7 3.1 %collective-permute-start.1 = (bf16[128,1792]{1,0:T(8,128)(2,1)S(1)}, bf16[128,1792]{1,0:T(8,128)(2,1)S(1)}, u32[]{:S(2)}, u32[]{:S(2)}) collective-permute-start(bf16[128,1792]{1,0:T(8,128)(2,1)S(1)} %pad_maximum_fusion.1), channel_id=1, source_target_pairs={{0,1},{1,0},{2,3},{3,2},{4,5},{5,4},{6,7},{7,6},{8,9},{9,8},{10,11... | collective-permute-start | bytes 1376264 | tf_op jit(solution)/shard_map/ppermute | solution.py:56
  108.8 0.9 fusion.48
  109.7 0.8 fusion.47
  110.6 0.7 constant_dynamic-update-slice_fusion.2
  111.3 0.7 constant_dynamic-update-slice_fusion.1
  112.0 6.8 %collective-permute-done.1 = bf16[128,1792]{1,0:T(8,128)(2,1)S(1)} collective-permute-done((bf16[128,1792]{1,0:T(8,128)(2,1)S(1)}, bf16[128,1792]{1,0:T(8,128)(2,1)S(1)}, u32[]{:S(2)}, u32[]{:S(2)}) %collective-permute-start.1) | collective-permute-done | bytes 458784 | tf_op jit(solution)/shard_map/ppermute | solution.py:56
  118.9 0.8 constant_dynamic-update-slice_fusion
  119.7 0.0 all-gather.2.cloned.1.call-update
  119.7 5.8 %constant_dynamic-slice_fusion.1 = (bf16[1024,896]{1,0:T(8,128)(2,1)S(1)}, bf16[1024,896]{1,0:T(8,128)(2,1)}, bf16[1024,896]{1,0:T(8,128)(2,1)}, bf16[1024,896]{1,0:T(8,128)(2,1)}) fusion(bf16[1024,1792]{1,0:T(8,128)(2,1)} %param.6, s32[]{:T(128)S(6)} %select_n.5, s32[]{:T(128)S(6)} %select_n.4, bf16[1024,1792]{1,0:T(8,128)(2,1)} %param.5), kind=kLoop, calls=%fused_computation.63 | loop fusion | bytes 14680072 | tf_op jit(solution)/shard_map/dynamic_slice | solution.py:8
  125.5 1.0 fusion.30
  126.6 54.8 %all-gather.2.cloned.1.call-done = bf16[1024,5376]{1,0:T(8,128)(2,1)} async-done(((bf16[128,5376]{1,0:T(8,128)(2,1)}), bf16[1024,5376]{1,0:T(8,128)(2,1)}) %all-gather.2.cloned.1.call-update) | async-done | bytes 11010064 | tf_op jit(solution)/shard_map/all_gather | solution.py:66
  181.3 12.9 %fusion.9 = bf16[1024,1024]{1,0:T(8,128)(2,1)} fusion(bf16[1024,896]{1,0:T(8,128)(2,1)} %get-tuple-element.29, bf16[1024,896]{1,0:T(8,128)(2,1)} %get-tuple-element.36, bf16[1024,896]{1,0:T(8,128)(2,1)S(1)} %get-tuple-element.28, bf16[1024,896]{1,0:T(8,128)(2,1)} %get-tuple-element.37, bf16[1024,5376]{1,0:T(8,128)(2,1)} %all-gather.2.cloned.1.call-done), kind=kOutput, calls=%fused_computation.14 | convolution fusion | flops 7546601472 | bytes 16777216 | tf_op jit(solution)/shard_map/dot_general | solution.py:75
  194.2 5.7 %all-to-all-start.2 = ((bf16[8,128,1024]{2,1,0:T(8,128)(2,1)}), bf16[8,128,1024]{2,1,0:T(8,128)(2,1)S(1)}, u32[]{:S(2)}, u32[]{:S(2)}) async-start(bf16[8,128,1024]{2,1,0:T(8,128)(2,1)} %bitcast.17), calls=%async_computation.3 | async-start | bytes 4194304 | tf_op jit(solution)/shard_map/all_to_all | solution.py:80
  200.0 4.7 %fusion.16 = bf16[1024,896]{1,0:T(8,128)(2,1)S(1)} fusion(bf16[1024,1024]{1,0:T(8,128)(2,1)} %bitcast.13, bf16[1024,5376]{1,0:T(8,128)(2,1)} %all-gather.2.cloned.1.call-done), kind=kOutput, calls=%fused_computation.17 | convolution fusion | flops 1879048192 | bytes 5767168 | tf_op jit(solution)/shard_map/dot_general | solution.py:84
  204.6 0.0 copy-done.3
  204.7 0.0 copy-start.5
  204.7 4.1 %fusion.20 = bf16[1024,896]{1,0:T(8,128)(2,1)S(1)} fusion(bf16[1024,1024]{1,0:T(8,128)(2,1)S(1)} %bitcast.14, bf16[1024,5376]{1,0:T(8,128)(2,1)} %all-gather.2.cloned.1.call-done), kind=kOutput, calls=%fused_computation.21 | convolution fusion | flops 1879048192 | bytes 5767168 | tf_op jit(solution)/shard_map/dot_general | solution.py:84
  208.7 0.0 copy-done.5
  208.8 5.2 %add_convert_fusion.1 = bf16[1024,896]{1,0:T(8,128)(2,1)} fusion(bf16[1024,896]{1,0:T(8,128)(2,1)S(1)} %fusion.20, bf16[1024,1024]{1,0:T(8,128)(2,1)S(1)} %bitcast.15, bf16[1024,5376]{1,0:T(8,128)(2,1)} %all-gather.2.cloned.1.call-done), kind=kOutput, calls=%fused_computation.13 | convolution fusion | flops 1883635712 | bytes 7602176 | tf_op jit(solution)/shard_map/dot_general | solution.py:85
  214.0 5.2 %add_convert_fusion = bf16[1024,896]{1,0:T(8,128)(2,1)} fusion(bf16[1024,896]{1,0:T(8,128)(2,1)S(1)} %fusion.16, bf16[1024,1024]{1,0:T(8,128)(2,1)S(1)} %bitcast.16, bf16[1024,5376]{1,0:T(8,128)(2,1)} %all-gather.2.cloned.1.call-done), kind=kOutput, calls=%fused_computation.12 | convolution fusion | flops 1883635712 | bytes 7602176 | tf_op jit(solution)/shard_map/dot_general | solution.py:85
  219.2 10.4 %all-to-all-done.2 = bf16[8,128,1024]{2,1,0:T(8,128)(2,1)S(1)} async-done(((bf16[8,128,1024]{2,1,0:T(8,128)(2,1)}), bf16[8,128,1024]{2,1,0:T(8,128)(2,1)S(1)}, u32[]{:S(2)}, u32[]{:S(2)}) %all-to-all-start.2) | async-done | bytes 2097184 | tf_op jit(solution)/shard_map/all_to_all | solution.py:80
  229.6 1.1 reduce_sum.12
  (6 shorter events, 0.1 us)
Async XLA Ops:
  7.2 96.9 %reduce-scatter.2.cloned.1.call-start = ((), (), s32[]{:S(2)}) async-start(), calls=%async_computation.4 | async-start | bytes 8257536 | tf_op jit(solution)/shard_map/reduce_scatter | solution.py:29
  8.4 30.9 %copy-start = (bf16[1024,1792]{1,0:T(8,128)(2,1)S(1)}, bf16[1024,1792]{1,0:T(8,128)(2,1)}, u32[]{:S(2)}) copy-start(bf16[1024,1792]{1,0:T(8,128)(2,1)} %param.6) | copy-start | bytes 11010052
  39.4 4.2 %copy-start.2 = (bf16[8,128,1024]{2,1,0:T(8,128)(2,1)}, bf16[8,128,1024]{2,1,0:T(8,128)(2,1)S(1)}, u32[]{:S(2)}) copy-start(bf16[8,128,1024]{2,1,0:T(8,128)(2,1)S(1)} %all_to_all.23) | copy-start | bytes 6291460
  39.4 4.2 %copy-start.1 = (bf16[1024,1792]{1,0:T(8,128)(2,1)S(1)}, bf16[1024,1792]{1,0:T(8,128)(2,1)}, u32[]{:S(2)}) copy-start(bf16[1024,1792]{1,0:T(8,128)(2,1)} %param.5) | copy-start | bytes 11010052
  54.5 0.9 copy-start.7
  55.4 8.1 %collective-permute-start = (bf16[128,1024]{1,0:T(8,128)(2,1)S(1)}, bf16[128,1024]{1,0:T(8,128)(2,1)S(1)}, u32[]{:S(2)}, u32[]{:S(2)}) collective-permute-start(bf16[128,1024]{1,0:T(8,128)(2,1)S(1)} %copy-done.7), channel_id=1, source_target_pairs={{0,1},{1,0},{2,3},{3,2},{4,5},{5,4},{6,7},{7,6},{8,9},{9,8},{10,11... | collective-permute-start | bytes 786440 | tf_op jit(solution)/shard_map/ppermute | solution.py:25
  65.1 5.9 %copy-start.6 = (bf16[128,1792]{1,0:T(8,128)(2,1)S(1)}, bf16[128,1792]{1,0:T(8,128)(2,1)}, u32[]{:S(2)}) copy-start(bf16[128,1792]{1,0:T(8,128)(2,1)} %param.7) | copy-start | bytes 1376260
  65.1 28.5 %all-to-all-start.1 = ((bf16[8,128,1024]{2,1,0:T(8,128)(2,1)}), bf16[8,128,1024]{2,1,0:T(8,128)(2,1)S(1)}, u32[]{:S(2)}, u32[]{:S(2)}) async-start(bf16[8,128,1024]{2,1,0:T(8,128)(2,1)} %tile.5), calls=%async_computation.2 | async-start | bytes 4194304 | tf_op jit(solution)/shard_map/all_to_all | solution.py:23
  71.1 110.3 %all-gather.2.cloned.1.call-start = ((), (), s32[]{:S(2)}) async-start(), calls=%async_computation.5 | async-start | bytes 12386304 | tf_op jit(solution)/shard_map/all_gather | solution.py:66
  93.7 10.4 %copy-start.4 = (bf16[8,128,1024]{2,1,0:T(8,128)(2,1)}, bf16[8,128,1024]{2,1,0:T(8,128)(2,1)S(1)}, u32[]{:S(2)}) copy-start(bf16[8,128,1024]{2,1,0:T(8,128)(2,1)S(1)} %all-to-all-done.1) | copy-start | bytes 6291460
  105.7 13.2 %collective-permute-start.1 = (bf16[128,1792]{1,0:T(8,128)(2,1)S(1)}, bf16[128,1792]{1,0:T(8,128)(2,1)S(1)}, u32[]{:S(2)}, u32[]{:S(2)}) collective-permute-start(bf16[128,1792]{1,0:T(8,128)(2,1)S(1)} %pad_maximum_fusion.1), channel_id=1, source_target_pairs={{0,1},{1,0},{2,3},{3,2},{4,5},{5,4},{6,7},{7,6},{8,9},{9,8},{10,11... | collective-permute-start | bytes 1376264 | tf_op jit(solution)/shard_map/ppermute | solution.py:56
  194.2 35.3 %all-to-all-start.2 = ((bf16[8,128,1024]{2,1,0:T(8,128)(2,1)}), bf16[8,128,1024]{2,1,0:T(8,128)(2,1)S(1)}, u32[]{:S(2)}, u32[]{:S(2)}) async-start(bf16[8,128,1024]{2,1,0:T(8,128)(2,1)} %bitcast.17), calls=%async_computation.3 | async-start | bytes 4194304 | tf_op jit(solution)/shard_map/all_to_all | solution.py:80
  200.0 4.7 %copy-start.3 = (bf16[8,128,1024]{2,1,0:T(8,128)(2,1)S(1)}, bf16[8,128,1024]{2,1,0:T(8,128)(2,1)}, u32[]{:S(2)}) copy-start(bf16[8,128,1024]{2,1,0:T(8,128)(2,1)} %copy-done.2) | copy-start | bytes 6291460
  204.7 4.1 %copy-start.5 = (bf16[8,128,1024]{2,1,0:T(8,128)(2,1)S(1)}, bf16[8,128,1024]{2,1,0:T(8,128)(2,1)}, u32[]{:S(2)}) copy-start(bf16[8,128,1024]{2,1,0:T(8,128)(2,1)} %copy-done.4) | copy-start | bytes 6291460
Sparse Core Ops, SparseCore 0:
  54.6 49.4 reduce-scatter.1
  119.9 61.4 all-gather.1
where the time goes:
time: 238 us
  waiting for transfers between devices  110 us (46%)
  matrix products  41.6 us (17%)
  blocking collectives  30.9 us (13%)
  starting transfers between devices  17.7 us (7%)
  between operations  14.2 us (6%)
  local copies, waits for them, and re-layouts  13.2 us (6%)
  other arithmetic  9.78 us (4%)
    all_gather x1, waiting for transfers between devices, on_device(): lax.all_gather(jnp.concatenate([gate_own, up_own, gate_other, up_other, p...  54.8 us
    all_to_all x1, blocking collectives, gather_col(): return lax.all_to_all(jnp.tile(block, (n_col, 1)), 'col', 0, 0, tiled=True)  30.9 us
    all_to_all x1, waiting for transfers between devices, gather_col(): return lax.all_to_all(jnp.tile(block, (n_col, 1)), 'col', 0, 0, tiled=True)  22.6 us
    dot_general x1, matrix products, on_device(): lax.dot_general(full[:, :2 * width], weights, transposed, preferred_eleme...  12.9 us
    dot_general x2, matrix products, weight_grad(): lax.dot_general(gathered_partner, partner, contract, preferred_element_ty...  10.4 us
    reduce_scatter x1, waiting for transfers between devices, on_device(): lax.psum_scatter(jnp.concatenate([first, second], axis=1).astype(jnp.bflo...  10.4 us
    all_to_all x1, waiting for transfers between devices, on_device(): parts = lax.all_to_all(term, 'col', 0, 0, tiled=True)  10.4 us
    dot_general x2, matrix products, weight_grad(): lax.dot_general(gathered, own, contract, preferred_element_type=jnp.float32)  8.74 us
  transfers between devices with their start and end apart: 6, of which 6 were waited for; matrix products, arithmetic and copies ran while one was open for 13% of the time, Pallas kernels for 0%

commit v1 on v0

--- a/solution.py
+++ b/solution.py
@@ -2,6 +2,19 @@
 import jax.numpy as jnp
 from jax import lax
 from jax.sharding import PartitionSpec as P
+
+
+def gather_around(x, axis, dim):
+    ways = lax.axis_size(axis)
+    up = [(d, (d + 1) % ways) for d in range(ways)]
+    down = [(d, (d - 1) % ways) for d in range(ways)]
+    earlier, later = ([x], [x])
+    for _ in range(ways // 2):
+        earlier.append(lax.ppermute(earlier[-1], axis, up))
+    for _ in range((ways - 1) // 2):
+        later.append(lax.ppermute(later[-1], axis, down))
+    line = jnp.concatenate([*earlier[::-1], *later[1:]], axis=dim)
+    return jnp.roll(line, (lax.axis_index(axis) - ways // 2) * x.shape[dim], axis=dim)
 
 
 def halves(x, dep, half):
@@ -63,11 +76,10 @@
         grad_gate_other,
         grad_up_other,
     )
-    full = lax.all_gather(
+    full = gather_around(
         jnp.concatenate([gate_own, up_own, gate_other, up_other, partner_gate, partner_up], axis=1),
         "row",
-        axis=0,
-        tiled=True,
+        0,
     )
     wg_own, wg_other = halves(gate_weight, dep, half)
     wu_own, wu_other = halves(up_weight, dep, half)

time: 238 us -> 272 us (1.14); the launches traced: 238 us -> 267 us
  local copies, waits for them, and re-layouts: 13.2 us -> 30.9 us
  starting transfers between devices: 17.7 us -> 26.3 us
    ppermute x0 -> x7, waiting for transfers between devices: none -> 62.4 us  [the longest x4 62.4 us: gather_around(): earlier.append(lax.ppermute(earlier[-1], axis, up))]
    all_gather x1 -> x0, waiting for transfers between devices: 54.8 us -> none  [on_device(): lax.all_gather(jnp.concatenate([gate_own, up_own, gate_other, up_other, p...]
    unnamed x18 -> x55, local copies, waits for them, and re-layouts: 2.41 us -> 22.7 us
    all_to_all x1, waiting for transfers between devices: 10.4 us -> 1.14 us  [on_device(): parts = lax.all_to_all(term, 'col', 0, 0, tiled=True)]
    ppermute x0 -> x7, starting transfers between devices: none -> 8.84 us  [the longest x3 8.81 us: gather_around(): later.append(lax.ppermute(later[-1], axis, down))]
  transfers between devices with their start and end apart: 6 -> 12, of which waited for: 6 -> 9; matrix products, arithmetic and copies ran while one was open for 13% -> 12% of each run, Pallas kernels for 0% -> 0%
where the time goes in v1:
time: 272 us; the launch traced here: 267 us
  waiting for transfers between devices  111 us (41%)
  matrix products  41.8 us (15%)
  local copies, waits for them, and re-layouts  30.9 us (11%)
  blocking collectives  30.7 us (11%)
  starting transfers between devices  26.3 us (10%)
  between operations  14.4 us (5%)
  other arithmetic  12.1 us (4%)
    ppermute x4, waiting for transfers between devices, gather_around(): earlier.append(lax.ppermute(earlier[-1], axis, up))  62.4 us
    all_to_all x1, blocking collectives, gather_col(): return lax.all_to_all(jnp.tile(block, (n_col, 1)), 'col', 0, 0, tiled=True)  30.7 us
    unnamed x55, local copies, waits for them, and re-layouts  22.7 us
    all_to_all x1, waiting for transfers between devices, gather_col(): return lax.all_to_all(jnp.tile(block, (n_col, 1)), 'col', 0, 0, tiled=True)  22.6 us
    dot_general x1, matrix products, on_device(): lax.dot_general(full[:, :2 * width], weights, transposed, preferred_eleme...  12.1 us
    reduce_scatter x1, waiting for transfers between devices, on_device(): lax.psum_scatter(jnp.concatenate([first, second], axis=1).astype(jnp.bflo...  10.6 us
    dot_general x2, matrix products, weight_grad(): lax.dot_general(gathered_partner, partner, contract, preferred_element_ty...  10.4 us
    ppermute x1, waiting for transfers between devices, on_device(): lax.ppermute(payload, 'dep', pair)  8.94 us
  transfers between devices with their start and end apart: 12, of which 9 were waited for; matrix products, arithmetic and copies ran while one was open for 12% of the time, Pallas kernels for 0%

profile of v1, /device:TPU:6, one launch (start us, length us, event | category | flops | bytes accessed | tf_op | source)
XLA Modules:
  0.0 267.0 jit_solution(7506856482674438950)
XLA Ops:
  7.2 1.4 tile.4
  8.6 30.7 %all_to_all.23 = bf16[8,128,1024]{2,1,0:T(8,128)(2,1)S(1)} all-to-all(bf16[8,128,1024]{2,1,0:T(8,128)(2,1)S(1)} %tile.4), channel_id=1, replica_groups=mesh['row'=8,'col'=8,'dep'=2] {'col'}, dimensions={0} | all-to-all | bytes 4194304 | tf_op jit(solution)/shard_map/all_to_all | solution.py:36
  39.2 5.4 %convolution_convert_fusion = bf16[1024,1792]{1,0:T(8,128)(2,1)} fusion(bf16[1024,1024]{1,0:T(8,128)(2,1)S(1)} %bitcast.13, bf16[1024,1792]{1,0:T(8,128)(2,1)S(1)} %copy-done.8), kind=kOutput, calls=%fused_computation.10 | convolution fusion | flops 3759931392 | bytes 9437184 | tf_op jit(solution)/shard_map/dot_general | solution.py:41
  44.6 5.4 %convolution_convert_fusion.1 = bf16[1024,1792]{1,0:T(8,128)(2,1)} fusion(bf16[1024,1024]{1,0:T(8,128)(2,1)S(1)} %bitcast.14, bf16[1024,1792]{1,0:T(8,128)(2,1)S(1)} %copy-done.9), kind=kOutput, calls=%fused_computation.11 | convolution fusion | flops 3759931392 | bytes 9437184 | tf_op jit(solution)/shard_map/dot_general | solution.py:40
  50.0 6.6 %pad_maximum_fusion = bf16[1024,3584]{1,0:T(8,128)(2,1)} fusion(bf16[1024,1792]{1,0:T(8,128)(2,1)} %convolution_convert_fusion, bf16[1024,1792]{1,0:T(8,128)(2,1)} %convolution_convert_fusion.1), kind=kLoop, calls=%fused_computation.2 | loop fusion | flops 14680064 | bytes 14680064 | tf_op jit(solution)/shard_map/concatenate | solution.py:43
  56.6 0.9 copy-done.15
  57.6 2.9 %collective-permute-start = (bf16[128,1024]{1,0:T(8,128)(2,1)S(1)}, bf16[128,1024]{1,0:T(8,128)(2,1)S(1)}, u32[]{:S(2)}, u32[]{:S(2)}) collective-permute-start(bf16[128,1024]{1,0:T(8,128)(2,1)S(1)} %copy-done.15), channel_id=1, source_target_pairs={{0,1},{1,0},{2,3},{3,2},{4,5},{5,4},{6,7},{7,6},{8,9},{9,8},{10,11... | collective-permute-start | bytes 786440 | tf_op jit(solution)/shard_map/ppermute | solution.py:38
  60.5 5.2 %collective-permute-done = bf16[128,1024]{1,0:T(8,128)(2,1)S(1)} collective-permute-done((bf16[128,1024]{1,0:T(8,128)(2,1)S(1)}, bf16[128,1024]{1,0:T(8,128)(2,1)S(1)}, u32[]{:S(2)}, u32[]{:S(2)}) %collective-permute-start) | collective-permute-done | bytes 262176 | tf_op jit(solution)/shard_map/ppermute | solution.py:38
  65.6 1.7 tile.5
  67.3 5.8 %all-to-all-start.1 = ((bf16[8,128,1024]{2,1,0:T(8,128)(2,1)}), bf16[8,128,1024]{2,1,0:T(8,128)(2,1)S(1)}, u32[]{:S(2)}, u32[]{:S(2)}) async-start(bf16[8,128,1024]{2,1,0:T(8,128)(2,1)} %tile.5), calls=%async_computation.2 | async-start | bytes 4194304 | tf_op jit(solution)/shard_map/all_to_all | solution.py:36
  73.1 22.6 %all-to-all-done.1 = bf16[8,128,1024]{2,1,0:T(8,128)(2,1)S(1)} async-done(((bf16[8,128,1024]{2,1,0:T(8,128)(2,1)}), bf16[8,128,1024]{2,1,0:T(8,128)(2,1)S(1)}, u32[]{:S(2)}, u32[]{:S(2)}) %all-to-all-start.1) | async-done | bytes 2097184 | tf_op jit(solution)/shard_map/all_to_all | solution.py:36
  95.7 10.6 %reduce-scatter.2.cloned.1.call-done = bf16[128,3584]{1,0:T(8,128)(2,1)} async-done(((bf16[1024,3584]{1,0:T(8,128)(2,1)}), bf16[128,3584]{1,0:T(8,128)(2,1)}) %reduce-scatter.2.cloned.1.call-update) | async-done | bytes 917520 | tf_op jit(solution)/shard_map/reduce_scatter | solution.py:42
  106.2 1.2 fusion.51
  107.5 0.3 fusion.33
  107.8 3.1 %collective-permute-start.1 = (bf16[128,1792]{1,0:T(8,128)(2,1)S(1)}, bf16[128,1792]{1,0:T(8,128)(2,1)S(1)}, u32[]{:S(2)}, u32[]{:S(2)}) collective-permute-start(bf16[128,1792]{1,0:T(8,128)(2,1)S(1)} %pad_maximum_fusion.1), channel_id=1, source_target_pairs={{0,1},{1,0},{2,3},{3,2},{4,5},{5,4},{6,7},{7,6},{8,9},{9,8},{10,11... | collective-permute-start | bytes 1376264 | tf_op jit(solution)/shard_map/ppermute | solution.py:69
  110.9 0.9 constant_dynamic-update-slice_fusion.4
  111.8 0.2 constant_dynamic-update-slice_fusion.3
  112.1 8.9 %collective-permute-done.1 = bf16[128,1792]{1,0:T(8,128)(2,1)S(1)} collective-permute-done((bf16[128,1792]{1,0:T(8,128)(2,1)S(1)}, bf16[128,1792]{1,0:T(8,128)(2,1)S(1)}, u32[]{:S(2)}, u32[]{:S(2)}) %collective-permute-start.1) | collective-permute-done | bytes 458784 | tf_op jit(solution)/shard_map/ppermute | solution.py:69
  121.1 18.9 %collective-permute-done.2 = bf16[128,5376]{1,0:T(8,128)(2,1)S(1)} collective-permute-done((bf16[128,5376]{1,0:T(8,128)(2,1)S(1)}, bf16[128,5376]{1,0:T(8,128)(2,1)S(1)}, u32[]{:S(2)}, u32[]{:S(2)}) %collective-permute-start.2) | collective-permute-done | bytes 1376288 | tf_op jit(solution)/shard_map/ppermute | solution.py:13
  140.0 1.1 copy-done
  141.1 3.0 %collective-permute-start.6 = (bf16[128,5376]{1,0:T(8,128)(2,1)S(1)}, bf16[128,5376]{1,0:T(8,128)(2,1)}, u32[]{:S(2)}, u32[]{:S(2)}) collective-permute-start(bf16[128,5376]{1,0:T(8,128)(2,1)S(1)} %constant_dynamic-update-slice_fusion), channel_id=1, source_target_pairs={{0,112},{16,0},{32,16},{48,32},{64,48},{80,64},{96,80},{112,96},{1... | collective-permute-start | bytes 4128776 | tf_op jit(solution)/shard_map/ppermute | solution.py:15
  144.0 16.0 %collective-permute-done.3 = bf16[128,5376]{1,0:T(8,128)(2,1)S(1)} collective-permute-done((bf16[128,5376]{1,0:T(8,128)(2,1)S(1)}, bf16[128,5376]{1,0:T(8,128)(2,1)S(1)}, u32[]{:S(2)}, u32[]{:S(2)}) %collective-permute-start.3) | collective-permute-done | bytes 1376288 | tf_op jit(solution)/shard_map/ppermute | solution.py:13
  160.0 1.1 copy-done.2
  161.1 3.0 %collective-permute-start.7 = (bf16[128,5376]{1,0:T(8,128)(2,1)}, bf16[128,5376]{1,0:T(8,128)(2,1)}, u32[]{:S(2)}, u32[]{:S(2)}) collective-permute-start(bf16[128,5376]{1,0:T(8,128)(2,1)} %collective-permute-done.6), channel_id=1, source_target_pairs={{0,112},{16,0},{32,16},{48,32},{64,48},{80,64},{96,80},{112,96},{1... | collective-permute-start | bytes 4128776 | tf_op jit(solution)/shard_map/ppermute | solution.py:15
  164.1 16.1 %collective-permute-done.4 = bf16[128,5376]{1,0:T(8,128)(2,1)} collective-permute-done((bf16[128,5376]{1,0:T(8,128)(2,1)S(1)}, bf16[128,5376]{1,0:T(8,128)(2,1)}, u32[]{:S(2)}, u32[]{:S(2)}) %collective-permute-start.4) | collective-permute-done | bytes 1376288 | tf_op jit(solution)/shard_map/ppermute | solution.py:13
  180.2 3.8 %constant_dynamic-slice_fusion.2 = (bf16[1024,896]{1,0:T(8,128)(2,1)S(1)}, bf16[1024,896]{1,0:T(8,128)(2,1)S(1)}, bf16[1024,896]{1,0:T(8,128)(2,1)S(1)}, bf16[1024,896]{1,0:T(8,128)(2,1)S(1)}) fusion(bf16[1024,1792]{1,0:T(8,128)(2,1)} %param.6, s32[]{:T(128)S(6)} %select_n.28, s32[]{:T(128)S(6)} %select_n.27, bf16[1024,1792]{1,0:T(8,128)(2,1)} %param.5), kind=kLoop, calls=%fused_computation.90 | loop fusion | bytes 14680072 | tf_op jit(solution)/shard_map/dynamic_slice | solution.py:21
  184.1 1.1 fusion.30
  185.1 2.9 %collective-permute-start.8 = (bf16[128,5376]{1,0:T(8,128)(2,1)}, bf16[128,5376]{1,0:T(8,128)(2,1)S(1)}, u32[]{:S(2)}, u32[]{:S(2)}) collective-permute-start(bf16[128,5376]{1,0:T(8,128)(2,1)} %collective-permute-done.7), channel_id=1, source_target_pairs={{0,112},{16,0},{32,16},{48,32},{64,48},{80,64},{96,80},{112,96},{1... | collective-permute-start | bytes 4128776 | tf_op jit(solution)/shard_map/ppermute | solution.py:15
  188.0 11.4 %collective-permute-done.5 = bf16[128,5376]{1,0:T(8,128)(2,1)} collective-permute-done((bf16[128,5376]{1,0:T(8,128)(2,1)}, bf16[128,5376]{1,0:T(8,128)(2,1)}, u32[]{:S(2)}, u32[]{:S(2)}) %collective-permute-start.5) | collective-permute-done | bytes 1376288 | tf_op jit(solution)/shard_map/ppermute | solution.py:13
  199.4 1.4 constant_dynamic-update-slice_fusion.20
  200.9 1.5 constant_dynamic-update-slice_fusion.19
  202.6 0.2 constant_dynamic-update-slice_fusion.28
  202.9 1.4 constant_dynamic-update-slice_fusion.15
  204.3 1.4 constant_dynamic-update-slice_fusion.14
  205.8 1.4 constant_dynamic-update-slice_fusion.12
  207.3 1.4 constant_dynamic-update-slice_fusion.11
  208.9 0.2 constant_dynamic-update-slice_fusion.24
  209.2 1.4 constant_dynamic-update-slice_fusion.7
  210.7 1.4 constant_dynamic-update-slice_fusion.6
  212.2 7.3 %copy-done.13 = bf16[2048,5376]{1,0:T(8,128)(2,1)} copy-done((bf16[2048,5376]{1,0:T(8,128)(2,1)}, bf16[2048,5376]{1,0:T(8,128)(2,1)S(1)}, u32[]{:S(2)}) %copy-start.13) | copy-done | bytes 22020120
  219.5 12.1 %fusion.9 = bf16[1024,1024]{1,0:T(8,128)(2,1)} fusion(bf16[1024,896]{1,0:T(8,128)(2,1)S(1)} %get-tuple-element.31, bf16[1024,896]{1,0:T(8,128)(2,1)S(1)} %get-tuple-element.38, bf16[1024,896]{1,0:T(8,128)(2,1)S(1)} %get-tuple-element.30, bf16[1024,896]{1,0:T(8,128)(2,1)S(1)} %get-tuple-element.39, bf16[2048,5376]{1,0:T(8,128)(2,1)} %copy-done.13, ...), kind=kOutput, calls=%fused_computation.14 | convolution fusion | flops 7546601472 | bytes 16777220 | tf_op jit(solution)/shard_map/dot_general | solution.py:87
  231.6 5.7 %all-to-all-start.2 = ((bf16[8,128,1024]{2,1,0:T(8,128)(2,1)}), bf16[8,128,1024]{2,1,0:T(8,128)(2,1)}, u32[]{:S(2)}, u32[]{:S(2)}) async-start(bf16[8,128,1024]{2,1,0:T(8,128)(2,1)} %bitcast.17), calls=%async_computation.3 | async-start | bytes 4194304 | tf_op jit(solution)/shard_map/all_to_all | solution.py:92
  237.3 4.7 %fusion.20 = bf16[1024,896]{1,0:T(8,128)(2,1)S(1)} fusion(bf16[1024,1024]{1,0:T(8,128)(2,1)} %bitcast.15, bf16[2048,5376]{1,0:T(8,128)(2,1)} %copy-done.13, s32[]{:T(128)S(6)} %select_n.30), kind=kOutput, calls=%fused_computation.21 | convolution fusion | flops 1879048192 | bytes 5767172 | tf_op jit(solution)/shard_map/dot_general | solution.py:96
  242.0 3.9 %fusion.16 = bf16[1024,896]{1,0:T(8,128)(2,1)S(1)} fusion(bf16[1024,1024]{1,0:T(8,128)(2,1)S(1)} %bitcast.16, bf16[2048,5376]{1,0:T(8,128)(2,1)} %copy-done.13, s32[]{:T(128)S(6)} %select_n.30, s32[]{:T(128)S(6)} %add.60), kind=kOutput, calls=%fused_computation.17 | convolution fusion | flops 1879048192 | bytes 5767176 | tf_op jit(solution)/shard_map/dot_general | solution.py:96
  245.9 5.2 %add_convert_fusion = bf16[1024,896]{1,0:T(8,128)(2,1)} fusion(bf16[1024,896]{1,0:T(8,128)(2,1)S(1)} %fusion.16, bf16[1024,1024]{1,0:T(8,128)(2,1)S(1)} %bitcast.11, bf16[2048,5376]{1,0:T(8,128)(2,1)} %copy-done.13, s32[]{:T(128)S(6)} %select_n.30, s32[]{:T(128)S(6)} %add.61), kind=kOutput, calls=%fused_computation.12 | convolution fusion | flops 1883635712 | bytes 7602184 | tf_op jit(solution)/shard_map/dot_general | solution.py:97
  251.1 5.2 %add_convert_fusion.1 = bf16[1024,896]{1,0:T(8,128)(2,1)} fusion(bf16[1024,896]{1,0:T(8,128)(2,1)S(1)} %fusion.20, bf16[1024,1024]{1,0:T(8,128)(2,1)S(1)} %bitcast.12, bf16[2048,5376]{1,0:T(8,128)(2,1)} %copy-done.13, s32[]{:T(128)S(6)} %select_n.30, s32[]{:T(128)S(6)} %add.59), kind=kOutput, calls=%fused_computation.13 | convolution fusion | flops 1883635712 | bytes 7602184 | tf_op jit(solution)/shard_map/dot_general | solution.py:97
  256.3 1.1 all-to-all-done.2
  257.4 2.7 %reduce_sum.12 = bf16[128,1024]{1,0:T(8,128)(2,1)} reduce(bf16[8,128,1024]{2,1,0:T(8,128)(2,1)} %all-to-all-done.2, bf16[]{:T(256)} %constant.49.clone.1), dimensions={0}, to_apply=%region_1.2 | reduce | flops 917504 | bytes 2359298 | tf_op jit(solution)/shard_map/reduce_sum | solution.py:93
  (57 shorter events, 1.1 us)
Async XLA Ops:
  7.2 99.1 %reduce-scatter.2.cloned.1.call-start = ((), (), s32[]{:S(2)}) async-start(), calls=%async_computation.4 | async-start | bytes 8257536 | tf_op jit(solution)/shard_map/reduce_scatter | solution.py:42
  7.2 32.0 %copy-start.8 = (bf16[1024,1792]{1,0:T(8,128)(2,1)S(1)}, bf16[1024,1792]{1,0:T(8,128)(2,1)}, u32[]{:S(2)}) copy-start(bf16[1024,1792]{1,0:T(8,128)(2,1)} %param.6) | copy-start | bytes 11010052
  39.2 5.4 %copy-start.10 = (bf16[8,128,1024]{2,1,0:T(8,128)(2,1)}, bf16[8,128,1024]{2,1,0:T(8,128)(2,1)S(1)}, u32[]{:S(2)}) copy-start(bf16[8,128,1024]{2,1,0:T(8,128)(2,1)S(1)} %all_to_all.23) | copy-start | bytes 6291460
  39.2 5.4 %copy-start.9 = (bf16[1024,1792]{1,0:T(8,128)(2,1)S(1)}, bf16[1024,1792]{1,0:T(8,128)(2,1)}, u32[]{:S(2)}) copy-start(bf16[1024,1792]{1,0:T(8,128)(2,1)} %param.5) | copy-start | bytes 11010052
  56.6 0.9 copy-start.15
  57.5 15.5 %copy-start.14 = (bf16[128,1792]{1,0:T(8,128)(2,1)S(1)}, bf16[128,1792]{1,0:T(8,128)(2,1)}, u32[]{:S(2)}) copy-start(bf16[128,1792]{1,0:T(8,128)(2,1)} %param.7) | copy-start | bytes 1376260
  57.6 8.1 %collective-permute-start = (bf16[128,1024]{1,0:T(8,128)(2,1)S(1)}, bf16[128,1024]{1,0:T(8,128)(2,1)S(1)}, u32[]{:S(2)}, u32[]{:S(2)}) collective-permute-start(bf16[128,1024]{1,0:T(8,128)(2,1)S(1)} %copy-done.15), channel_id=1, source_target_pairs={{0,1},{1,0},{2,3},{3,2},{4,5},{5,4},{6,7},{7,6},{8,9},{9,8},{10,11... | collective-permute-start | bytes 786440 | tf_op jit(solution)/shard_map/ppermute | solution.py:38
  67.3 28.4 %all-to-all-start.1 = ((bf16[8,128,1024]{2,1,0:T(8,128)(2,1)}), bf16[8,128,1024]{2,1,0:T(8,128)(2,1)S(1)}, u32[]{:S(2)}, u32[]{:S(2)}) async-start(bf16[8,128,1024]{2,1,0:T(8,128)(2,1)} %tile.5), calls=%async_computation.2 | async-start | bytes 4194304 | tf_op jit(solution)/shard_map/all_to_all | solution.py:36
  107.4 72.7 %copy-start.4 = (bf16[128,1792]{1,0:T(8,128)(2,1)}, bf16[128,1792]{1,0:T(8,128)(2,1)S(1)}, u32[]{:S(2)}) copy-start(bf16[128,1792]{1,0:T(8,128)(2,1)S(1)} %get-tuple-element.17) | copy-start | bytes 1376260
  107.5 72.7 %copy-start.6 = (bf16[128,1792]{1,0:T(8,128)(2,1)}, bf16[128,1792]{1,0:T(8,128)(2,1)S(1)}, u32[]{:S(2)}) copy-start(bf16[128,1792]{1,0:T(8,128)(2,1)S(1)} %get-tuple-element.16) | copy-start | bytes 1376260
  107.8 13.2 %collective-permute-start.1 = (bf16[128,1792]{1,0:T(8,128)(2,1)S(1)}, bf16[128,1792]{1,0:T(8,128)(2,1)S(1)}, u32[]{:S(2)}, u32[]{:S(2)}) collective-permute-start(bf16[128,1792]{1,0:T(8,128)(2,1)S(1)} %pad_maximum_fusion.1), channel_id=1, source_target_pairs={{0,1},{1,0},{2,3},{3,2},{4,5},{5,4},{6,7},{7,6},{8,9},{9,8},{10,11... | collective-permute-start | bytes 1376264 | tf_op jit(solution)/shard_map/ppermute | solution.py:69
  121.0 19.0 %collective-permute-start.2 = (bf16[128,5376]{1,0:T(8,128)(2,1)S(1)}, bf16[128,5376]{1,0:T(8,128)(2,1)S(1)}, u32[]{:S(2)}, u32[]{:S(2)}) collective-permute-start(bf16[128,5376]{1,0:T(8,128)(2,1)S(1)} %constant_dynamic-update-slice_fusion), channel_id=1, source_target_pairs={{0,16},{16,32},{32,48},{48,64},{64,80},{80,96},{96,112},{112,0},{1... | collective-permute-start | bytes 4128776 | tf_op jit(solution)/shard_map/ppermute | solution.py:13
  140.0 1.1 copy-start
  141.1 18.9 %collective-permute-start.3 = (bf16[128,5376]{1,0:T(8,128)(2,1)S(1)}, bf16[128,5376]{1,0:T(8,128)(2,1)S(1)}, u32[]{:S(2)}, u32[]{:S(2)}) collective-permute-start(bf16[128,5376]{1,0:T(8,128)(2,1)S(1)} %collective-permute-done.2), channel_id=1, source_target_pairs={{0,16},{16,32},{32,48},{48,64},{64,80},{80,96},{96,112},{112,0},{1... | collective-permute-start | bytes 4128776 | tf_op jit(solution)/shard_map/ppermute | solution.py:13
  141.1 20.0 %collective-permute-start.6 = (bf16[128,5376]{1,0:T(8,128)(2,1)S(1)}, bf16[128,5376]{1,0:T(8,128)(2,1)}, u32[]{:S(2)}, u32[]{:S(2)}) collective-permute-start(bf16[128,5376]{1,0:T(8,128)(2,1)S(1)} %constant_dynamic-update-slice_fusion), channel_id=1, source_target_pairs={{0,112},{16,0},{32,16},{48,32},{64,48},{80,64},{96,80},{112,96},{1... | collective-permute-start | bytes 4128776 | tf_op jit(solution)/shard_map/ppermute | solution.py:15
  160.0 1.1 copy-start.2
  161.1 19.1 %collective-permute-start.4 = (bf16[128,5376]{1,0:T(8,128)(2,1)S(1)}, bf16[128,5376]{1,0:T(8,128)(2,1)}, u32[]{:S(2)}, u32[]{:S(2)}) collective-permute-start(bf16[128,5376]{1,0:T(8,128)(2,1)S(1)} %collective-permute-done.3), channel_id=1, source_target_pairs={{0,16},{16,32},{32,48},{48,64},{64,80},{80,96},{96,112},{112,0},{1... | collective-permute-start | bytes 4128776 | tf_op jit(solution)/shard_map/ppermute | solution.py:13
  161.1 24.0 %collective-permute-start.7 = (bf16[128,5376]{1,0:T(8,128)(2,1)}, bf16[128,5376]{1,0:T(8,128)(2,1)}, u32[]{:S(2)}, u32[]{:S(2)}) collective-permute-start(bf16[128,5376]{1,0:T(8,128)(2,1)} %collective-permute-done.6), channel_id=1, source_target_pairs={{0,112},{16,0},{32,16},{48,32},{64,48},{80,64},{96,80},{112,96},{1... | collective-permute-start | bytes 4128776 | tf_op jit(solution)/shard_map/ppermute | solution.py:15
  180.2 19.3 %collective-permute-start.5 = (bf16[128,5376]{1,0:T(8,128)(2,1)}, bf16[128,5376]{1,0:T(8,128)(2,1)}, u32[]{:S(2)}, u32[]{:S(2)}) collective-permute-start(bf16[128,5376]{1,0:T(8,128)(2,1)} %collective-permute-done.4), channel_id=1, source_target_pairs={{0,16},{16,32},{32,48},{48,64},{64,80},{80,96},{96,112},{112,0},{1... | collective-permute-start | bytes 4128776 | tf_op jit(solution)/shard_map/ppermute | solution.py:13
  180.2 3.8 %copy-start.5 = (bf16[128,1792]{1,0:T(8,128)(2,1)S(1)}, bf16[128,1792]{1,0:T(8,128)(2,1)}, u32[]{:S(2)}) copy-start(bf16[128,1792]{1,0:T(8,128)(2,1)} %copy-done.4) | copy-start | bytes 1376260
  180.2 3.8 %copy-start.7 = (bf16[128,1792]{1,0:T(8,128)(2,1)S(1)}, bf16[128,1792]{1,0:T(8,128)(2,1)}, u32[]{:S(2)}) copy-start(bf16[128,1792]{1,0:T(8,128)(2,1)} %copy-done.6) | copy-start | bytes 1376260
  184.0 18.3 %copy-start.3 = (bf16[128,5376]{1,0:T(8,128)(2,1)S(1)}, bf16[128,5376]{1,0:T(8,128)(2,1)}, u32[]{:S(2)}) copy-start(bf16[128,5376]{1,0:T(8,128)(2,1)} %copy-done.2) | copy-start | bytes 4128772
  185.1 17.3 %copy-start.1 = (bf16[128,5376]{1,0:T(8,128)(2,1)S(1)}, bf16[128,5376]{1,0:T(8,128)(2,1)}, u32[]{:S(2)}) copy-start(bf16[128,5376]{1,0:T(8,128)(2,1)} %copy-done) | copy-start | bytes 4128772
  185.1 20.6 %collective-permute-start.8 = (bf16[128,5376]{1,0:T(8,128)(2,1)}, bf16[128,5376]{1,0:T(8,128)(2,1)S(1)}, u32[]{:S(2)}, u32[]{:S(2)}) collective-permute-start(bf16[128,5376]{1,0:T(8,128)(2,1)} %collective-permute-done.7), channel_id=1, source_target_pairs={{0,112},{16,0},{32,16},{48,32},{64,48},{80,64},{96,80},{112,96},{1... | collective-permute-start | bytes 4128776 | tf_op jit(solution)/shard_map/ppermute | solution.py:15
  200.8 1.7 copy-start.12
  212.2 7.3 %copy-start.13 = (bf16[2048,5376]{1,0:T(8,128)(2,1)}, bf16[2048,5376]{1,0:T(8,128)(2,1)S(1)}, u32[]{:S(2)}) copy-start(bf16[2048,5376]{1,0:T(8,128)(2,1)S(1)} %constant_dynamic-update-slice_fusion.5) | copy-start | bytes 66060292
  231.6 25.8 %all-to-all-start.2 = ((bf16[8,128,1024]{2,1,0:T(8,128)(2,1)}), bf16[8,128,1024]{2,1,0:T(8,128)(2,1)}, u32[]{:S(2)}, u32[]{:S(2)}) async-start(bf16[8,128,1024]{2,1,0:T(8,128)(2,1)} %bitcast.17), calls=%async_computation.3 | async-start | bytes 4194304 | tf_op jit(solution)/shard_map/all_to_all | solution.py:92
  237.3 4.7 %copy-start.11 = (bf16[8,128,1024]{2,1,0:T(8,128)(2,1)S(1)}, bf16[8,128,1024]{2,1,0:T(8,128)(2,1)}, u32[]{:S(2)}) copy-start(bf16[8,128,1024]{2,1,0:T(8,128)(2,1)} %copy-done.10) | copy-start | bytes 6291460
Sparse Core Ops, SparseCore 0:
  56.7 49.4 reduce-scatter.1
